TPU v7x, 32 devices: a whole 2x2x4 slice. The times are simulated.
32 devices in a mesh: groups: 2 (over y), dp: 4 (over z), mp: 4 (over x, core).
Axes of the slice: x: 2, y: 2, z: 4, core: 2. Of those that a mesh axis runs over, the one named last changes fastest.
Arguments:
- latents: bfloat16 [256, 640, 64], P(('groups', 'dp'), 'mp'), parts along dimension 0
- modulation: bfloat16 [256, 2, 640], P(('groups', 'dp'), None, 'mp'), parts along dimension 0, may hold values from -3 to 3
- first_kernel: bfloat16 [640, 9, 640], P('dp', None, 'mp'), may hold values from -0.078125 to 0.078125
- second_kernel: bfloat16 [640, 9, 640], P('dp', None, 'mp'), may hold values from -0.078125 to 0.078125
- encoder_cache: bfloat16 [336, 1280, 128], P(('groups', 'dp'), 'mp'), parts along dimension 0
- query_weight: bfloat16 [640, 640], P('dp'), may hold values from -0.25 to 0.25
- output_weight: bfloat16 [640, 640], P('dp'), may hold values from -0.25 to 0.25
- kept_prompt_list: int32 [256], P('groups'), parts along dimension 0, may hold values from 0 to 167, as said below
- destination: int32 [256], P('groups'), parts along dimension 0, may hold values from 0 to 3, as said below
- lengths: int32 [336], P('groups'), parts along dimension 0, may hold values from 1 to 128, 10752 in all
Outputs:
- level_out: bfloat16 [256, 640, 64], P(('groups', 'dp'), 'mp'), parts along dimension 0
There are 2 independent parts, one for each index of `groups`. A program takes and returns all parts, laid end to end along the dimension named above; an argument that names none is the same for every part. Nothing has to cross between parts.
Inputs may be any that keep to these rules, and one draw needn't show every extreme that they name: `kept_prompt_list`: entries o * 32 to o * 32 + 31 belong to owner o: distinct ids of its prompts o * 42 to o * 42 + 41. `destination`: names the shard of each survivor; every shard receives exactly 32 survivors, one owner sends at most 16 survivors to one shard, and every owner sends exactly 16 to some shard.
All inputs are finite; a program needn't handle non-finite values.
Results may differ from a plain program's by a relative error of at most 0.0055.
Values may be sent and summed in bfloat16 or wider, within the bound.
No kernel may reach another device: no remote copies, remote signals or barrier semaphores. Data moves between devices by JAX's collectives and lax.ppermute only.
A program may use at most 64 MiB of HBM per device.

v0:
```python
import jax
import jax.numpy as jnp
from jax import lax
from jax.sharding import PartitionSpec as P

C = 640
GROUPS = 32
HEAD = 64
SIDE = 8


EPSILON = 1e-05
MASKED = -1e30


def norm_groups(values, group_width):
    field_shape = values.shape
    grouped = values.reshape(
        field_shape[0], field_shape[1] // group_width, group_width, field_shape[2]
    )
    center = grouped - jnp.mean(grouped, axis=(2, 3), keepdims=True)
    spread = jnp.mean(center * center, axis=(2, 3), keepdims=True)
    return (center * lax.rsqrt(spread + EPSILON)).reshape(field_shape)


def gather_channels(field):
    return lax.all_gather(field, "mp", axis=1, tiled=True)


def gather_kernel(weight_shard):
    return lax.all_gather(weight_shard, "dp", axis=0, tiled=True)


def gather_projection(weight_shard):
    return lax.all_gather(weight_shard, "dp", axis=0, tiled=True)


def apply_kernel(full_field, kernel):
    sample_count = full_field.shape[0]
    out_width = kernel.shape[2]
    tap_images = jnp.einsum("scq,cte->steq", full_field, kernel, preferred_element_type=jnp.float32)
    tap_images = tap_images.reshape(sample_count, 9, out_width, SIDE, SIDE)
    padded = jnp.pad(tap_images, ((0, 0), (0, 0), (0, 0), (1, 1), (1, 1)))
    running = padded[:, 0, :, 0:SIDE, 0:SIDE]
    for offset in range(1, 9):
        row_shift, col_shift = (offset // 3, offset % 3)
        running = (
            running
            + padded[:, offset, :, row_shift : row_shift + SIDE, col_shift : col_shift + SIDE]
        )
    return running.reshape(sample_count, out_width, SIDE * SIDE)


def local(
    latents,
    modulation,
    first_kernel,
    second_kernel,
    encoder_cache,
    query_weight,
    output_weight,
    kept_prompt_list,
    destination,
    lengths,
):
    group_width = C // GROUPS
    dp_count = lax.axis_size("dp")
    mp_count = lax.axis_size("mp")
    my_shard = lax.axis_index("dp")
    my_column = lax.axis_index("mp")
    sample_shard_count = latents.shape[0]
    prompt_dev = encoder_cache.shape[0]
    cache_len = encoder_cache.shape[2]
    cache_width = encoder_cache.shape[1]
    cell_count = latents.shape[2]
    slot_limit = 2 * (sample_shard_count // dp_count)
    all_samples = destination.shape[0]
    owner_target = destination.reshape(dp_count, sample_shard_count)
    positions = jnp.arange(sample_shard_count, dtype=jnp.int32)
    before = positions[None, :] < positions[:, None]
    same_target = owner_target[:, :, None] == owner_target[:, None, :]
    slot_rank = jnp.sum((same_target & before[None]).astype(jnp.int32), axis=2)
    my_target = lax.dynamic_index_in_dim(owner_target, my_shard, 0, keepdims=False)
    my_rank = lax.dynamic_index_in_dim(slot_rank, my_shard, 0, keepdims=False)
    my_prompts = (
        lax.dynamic_slice_in_dim(
            kept_prompt_list, my_shard * sample_shard_count, sample_shard_count
        )
        - my_shard * prompt_dev
    )
    send_slot = my_target * slot_limit + my_rank
    slot_table = send_slot[:, None] == jnp.arange(dp_count * slot_limit, dtype=jnp.int32)[None, :]
    source_row = jnp.sum(jnp.where(slot_table, my_prompts[:, None], 0), axis=0)
    filled = jnp.any(slot_table, axis=0)
    send_rows = jnp.take(encoder_cache, source_row, axis=0)
    send_rows = jnp.where(filled[:, None, None], send_rows, jnp.zeros_like(send_rows))
    outgoing = send_rows.reshape(dp_count, slot_limit, cache_width, cache_len)
    incoming = lax.all_to_all(outgoing, "dp", split_axis=0, concat_axis=0, tiled=True)
    arriving = destination == my_shard
    arrival_pos = jnp.cumsum(arriving.astype(jnp.int32)) - 1
    selector = arriving[None, :] & (arrival_pos[None, :] == positions[:, None])
    kept_prompt = jnp.sum(
        jnp.where(selector, jnp.arange(all_samples, dtype=jnp.int32)[None, :], 0), axis=1
    )
    incoming_order_rank = jnp.sum(jnp.where(selector, slot_rank.reshape(-1)[None, :], 0), axis=1)
    prompt_ids = jnp.sum(jnp.where(selector, kept_prompt_list[None, :], 0), axis=1)
    landing_slot = kept_prompt // sample_shard_count * slot_limit + incoming_order_rank
    my_pairs = jnp.take(
        incoming.reshape(dp_count * slot_limit, cache_width, cache_len), landing_slot, axis=0
    )
    prompt_hits = prompt_ids[:, None] == jnp.arange(lengths.shape[0], dtype=jnp.int32)[None, :]
    my_lengths = jnp.sum(jnp.where(prompt_hits, lengths[None, :], 0), axis=1)
    start_field = latents.astype(jnp.float32)
    activated = jax.nn.silu(norm_groups(start_field, group_width)).astype(jnp.bfloat16)
    first_in = gather_channels(activated)
    weight_shards = (first_kernel, second_kernel, query_weight, output_weight)

    def convolve(full_field, which_weight):
        return apply_kernel(full_field, gather_kernel(weight_shards[which_weight]))

    def project(field_rows, which_weight):
        full_weight = gather_projection(weight_shards[which_weight])
        return jnp.einsum(
            "scq,ce->seq", field_rows, full_weight, preferred_element_type=jnp.float32
        )

    first_out = convolve(first_in, 0)
    scale_term = modulation[:, 0, :].astype(jnp.float32)[:, :, None]
    shift_term = modulation[:, 1, :].astype(jnp.float32)[:, :, None]
    modulated = jax.nn.silu(
        norm_groups(first_out, group_width) * (1.0 + scale_term) + shift_term
    ).astype(jnp.bfloat16)
    second_in = gather_channels(modulated)
    residual = start_field + convolve(second_in, 1)
    normed_out = norm_groups(residual, group_width).astype(jnp.bfloat16)
    local_samples = sample_shard_count // mp_count
    query_cells, pair_heads = (
        lax.all_to_all(normed_out, "mp", split_axis=0, concat_axis=1, tiled=True),
        lax.all_to_all(my_pairs, "mp", split_axis=0, concat_axis=1, tiled=True),
    )
    total_width = query_cells.shape[1]
    head_count = total_width // HEAD
    queries = project(query_cells, 2).astype(jnp.bfloat16)
    queries = queries.reshape(local_samples, head_count, HEAD, cell_count)
    heads_of_keys = pair_heads[:, :total_width, :].reshape(
        local_samples, head_count, HEAD, cache_len
    )
    value_heads = pair_heads[:, total_width:, :].reshape(local_samples, head_count, HEAD, cache_len)
    scores = jnp.einsum(
        "shdq,shdk->shqk", queries, heads_of_keys, preferred_element_type=jnp.float32
    ) * HEAD ** (-0.5)
    local_lengths = lax.dynamic_slice_in_dim(my_lengths, my_column * local_samples, local_samples)
    visible = (
        jnp.arange(cache_len, dtype=jnp.int32)[None, None, None, :]
        < local_lengths[:, None, None, None]
    )
    scores = jnp.where(visible, scores, MASKED)
    row_peak = jnp.max(scores, axis=3, keepdims=True)
    exponent = jnp.exp(scores - row_peak)
    attention = (exponent / jnp.sum(exponent, axis=3, keepdims=True)).astype(jnp.bfloat16)
    context = jnp.einsum(
        "shqk,shdk->shdq", attention, value_heads, preferred_element_type=jnp.float32
    ).astype(jnp.bfloat16)
    attended = project(context.reshape(local_samples, total_width, cell_count), 3).astype(
        jnp.bfloat16
    )
    returned = lax.all_to_all(attended, "mp", split_axis=1, concat_axis=0, tiled=True)
    final_field = residual + returned.astype(jnp.float32)
    return final_field.astype(jnp.bfloat16)


def solution(mesh):
    in_specs = (
        P(("groups", "dp"), "mp", None),
        P(("groups", "dp"), None, "mp"),
        P("dp", None, "mp"),
        P("dp", None, "mp"),
        P(("groups", "dp"), "mp", None),
        P("dp", None),
        P("dp", None),
        P("groups"),
        P("groups"),
        P("groups"),
    )
    out_specs = P(("groups", "dp"), "mp", None)
    return jax.shard_map(local, mesh=mesh, in_specs=in_specs, out_specs=out_specs, check_vma=False)
```

profile of v0, /device:TPU:0, one launch (start us, length us, event | category | flops | bytes accessed | tf_op | source)
XLA Modules:
  0.0 410.8 jit_solution(1955617540782185775)
XLA Ops:
  7.3 1.7 convert_reduce_fusion
  17.7 2.9 fusion.28
  20.6 3.0 copy.83
  24.5 3.5 gather_fusion
  28.1 5.6 %select_select_fusion = bf16[4,16,320,128]{3,2,1,0:T(8,128)(2,1)} fusion(bf16[4,16,320,128]{3,2,1,0:T(8,128)(2,1)} %bitcast.103, pred[4,16]{1,0:T(4,128)(4,1)S(1)} %compare_and_fusion, pred[4,16]{1,0:T(4,128)(4,1)S(1)} %broadcast_in_dim.127), kind=kLoop, calls=%fused_computation.23 | loop fusion | flops 5242880 | bytes 10485888 | tf_op jit(solution)/shard_map/jit(_where)/select_n | solution.py:96
  33.6 6.4 %all-to-all-start = ((bf16[4,16,320,128]{3,2,1,0:T(8,128)(2,1)}), bf16[4,16,320,128]{3,2,1,0:T(8,128)(2,1)}, u32[]{:S(2)}, u32[]{:S(2)}) async-start(bf16[4,16,320,128]{3,2,1,0:T(8,128)(2,1)} %select_select_fusion), calls=%async_computation | async-start | bytes 10485760 | tf_op jit(solution)/shard_map/all_to_all | solution.py:98
  40.9 72.6 %all-gather.7.cloned.1.call-done = bf16[640,9,160]{2,0,1:T(8,128)(2,1)} async-done(((bf16[160,9,160]{2,0,1:T(8,128)(2,1)}), bf16[640,9,160]{2,0,1:T(8,128)(2,1)}) %all-gather.7.cloned.1.call-update) | async-done | bytes 1843216 | tf_op jit(solution)/shard_map/all_gather | solution.py:31
  113.5 40.1 %all-gather.5.cloned.1.call-done = bf16[32,640,64]{2,0,1:T(8,128)(2,1)} async-done(((bf16[32,160,64]{2,0,1:T(8,128)(2,1)}), bf16[32,640,64]{2,0,1:T(8,128)(2,1)}) %all-gather.5.cloned.1.call-update) | async-done | bytes 2621456 | tf_op jit(solution)/shard_map/all_gather | solution.py:27
  153.6 11.1 %convolution_bitcast_fusion.1 = f32[32,9,160,8,8]{2,4,3,1,0:T(8,128)S(1)} fusion(bf16[32,640,64,1]{2,0,1,3:T(8,128)(2,1)} %bitcast.106, bf16[640,9,160]{2,0,1:T(8,128)(2,1)} %all-gather.7.cloned.1.call-done), kind=kOutput, calls=%fused_computation.20 | convolution fusion | flops 3774873600 | bytes 16261120 | tf_op jit(solution)/shard_map/scq,cte->steq/dot_general | solution.py:41
  164.8 2.3 fusion.58
  169.1 2.0 copy.87
  171.8 60.1 %all-gather.11.cloned.1.call-done = bf16[640,9,160]{2,0,1:T(8,128)(2,1)} async-done(((bf16[160,9,160]{2,0,1:T(8,128)(2,1)}), bf16[640,9,160]{2,0,1:T(8,128)(2,1)}) %all-gather.11.cloned.1.call-update) | async-done | bytes 1843216 | tf_op jit(solution)/shard_map/all_gather | solution.py:31
  231.9 40.4 %all-gather.9.cloned.1.call-done = bf16[32,640,64]{2,0,1:T(8,128)(2,1)} async-done(((bf16[32,160,64]{2,0,1:T(8,128)(2,1)}), bf16[32,640,64]{2,0,1:T(8,128)(2,1)}) %all-gather.9.cloned.1.call-update) | async-done | bytes 2621456 | tf_op jit(solution)/shard_map/all_gather | solution.py:27
  272.3 11.2 %convolution_bitcast_fusion = f32[32,9,160,8,8]{2,4,3,1,0:T(8,128)S(1)} fusion(bf16[32,640,64,1]{2,0,1,3:T(8,128)(2,1)} %bitcast.107, bf16[640,9,160]{2,0,1:T(8,128)(2,1)} %all-gather.11.cloned.1.call-done), kind=kOutput, calls=%fused_computation.19 | convolution fusion | flops 3774873600 | bytes 16261120 | tf_op jit(solution)/shard_map/scq,cte->steq/dot_general | solution.py:41
  283.5 2.7 fusion.57
  288.8 4.3 %all-to-all-start.2 = ((bf16[32,160,64]{1,2,0:T(8,128)(2,1)}), bf16[32,160,64]{1,2,0:T(8,128)(2,1)}, u32[]{:S(2)}, u32[]{:S(2)}) async-start(bf16[32,160,64]{1,2,0:T(8,128)(2,1)} %multiply_convert_fusion), calls=%async_computation.2 | async-start | bytes 2097152 | tf_op jit(solution)/shard_map/all_to_all | solution.py:138
  293.1 3.5 gather_fusion.1
  296.6 1.8 broadcast_select_fusion
  298.4 9.1 %all-to-all-done.2 = bf16[32,160,64]{1,2,0:T(8,128)(2,1)} async-done(((bf16[32,160,64]{1,2,0:T(8,128)(2,1)}), bf16[32,160,64]{1,2,0:T(8,128)(2,1)}, u32[]{:S(2)}, u32[]{:S(2)}) %all-to-all-start.2) | async-done | bytes 655392 | tf_op jit(solution)/shard_map/all_to_all | solution.py:138
  307.6 3.7 all-to-all-start.1
  311.6 20.3 %all_gather.22 = bf16[640,640]{1,0:T(8,128)(2,1)} all-gather(bf16[160,640]{1,0:T(8,128)(2,1)S(1)} %copy-done.5), channel_id=1, replica_groups=mesh['groups'=2,'dp'=4,'mp'=4] {'dp'}, dimensions={0}, use_global_device_ids=true | all-gather | bytes 1024000 | tf_op jit(solution)/shard_map/all_gather | solution.py:35
  331.9 18.9 %all_gather.23 = bf16[640,640]{1,0:T(8,128)(2,1)S(1)} all-gather(bf16[160,640]{1,0:T(8,128)(2,1)} %param.16), channel_id=1, replica_groups=mesh['groups'=2,'dp'=4,'mp'=4] {'dp'}, dimensions={0}, use_global_device_ids=true | all-gather | bytes 1024000 | tf_op jit(solution)/shard_map/all_gather | solution.py:35
  350.8 3.0 copy.116
  353.8 2.9 all_to_all.44
  356.7 2.9 fusion.39
  359.6 2.3 copy.92
  363.9 2.1 fusion.63
  366.0 1.9 fusion.62
  367.9 11.1 %convolution_convert_fusion = bf16[8,10,64,64]{3,2,1,0:T(8,128)(2,1)S(1)} fusion(bf16[8,10,64,128]{3,2,1,0:T(8,128)(2,1)} %bitcast.115, f32[8,10,64]{2,1,0:T(8,128)S(1)} %fusion.62, f32[8,10,64,128]{3,2,1,0:T(8,128)} %fusion.63, pred[8,128]{1,0:T(8,128)(4,1)S(1)} %iota_compare_fusion.4), kind=kOutput, calls=%fused_computation.69 | convolution fusion | flops 87495808 | bytes 4609024 | tf_op jit(solution)/shard_map/shqk,shdk->shdq/dot_general | solution.py:161
  382.2 13.2 %all_to_all.50 = bf16[4,2,40960]{2,1,0:T(2,128)(2,1)S(1)} all-to-all(bf16[4,2,40960]{2,1,0:T(2,128)(2,1)S(1)} %reshape.361), channel_id=1, replica_groups=mesh['groups'=2,'dp'=4,'mp'=4] {'mp'}, dimensions={0} | all-to-all | bytes 1310720 | tf_op jit(solution)/shard_map/all_to_all | solution.py:167
  397.2 3.5 copy.96
  400.7 3.5 fusion.30
  (98 shorter events, 23.2 us)
Async XLA Ops:
  6.5 18.0 %copy-start = (bf16[42,320,128]{2,1,0:T(8,128)(2,1)S(1)}, bf16[42,320,128]{2,1,0:T(8,128)(2,1)}, u32[]{:S(2)}) copy-start(bf16[42,320,128]{2,1,0:T(8,128)(2,1)} %param.14) | copy-start | bytes 10321924
  6.5 107.0 %all-gather.7.cloned.1.call-start = ((), (), s32[]{:S(2)}) async-start(), calls=%async_computation.5 | async-start | bytes 3686400 | tf_op jit(solution)/shard_map/all_gather | solution.py:31
  7.3 146.4 %all-gather.5.cloned.1.call-start = ((), (), s32[]{:S(2)}) async-start(), calls=%async_computation.4 | async-start | bytes 6553600 | tf_op jit(solution)/shard_map/all_gather | solution.py:27
  20.6 3.1 copy-start.7
  20.6 3.4 copy-start.8
  33.6 7.2 %copy-start.6 = (bf16[32,2,160]{2,1,0:T(2,128)(2,1)S(1)}, bf16[32,2,160]{2,1,0:T(2,128)(2,1)}, u32[]{:S(2)}) copy-start(bf16[32,2,160]{2,1,0:T(2,128)(2,1)} %param.11) | copy-start | bytes 61444
  33.6 255.2 %all-to-all-start = ((bf16[4,16,320,128]{3,2,1,0:T(8,128)(2,1)}), bf16[4,16,320,128]{3,2,1,0:T(8,128)(2,1)}, u32[]{:S(2)}, u32[]{:S(2)}) async-start(bf16[4,16,320,128]{3,2,1,0:T(8,128)(2,1)} %select_select_fusion), calls=%async_computation | async-start | bytes 10485760 | tf_op jit(solution)/shard_map/all_to_all | solution.py:98
  40.1 191.8 %all-gather.11.cloned.1.call-start = ((), (), s32[]{:S(2)}) async-start(), calls=%async_computation.7 | async-start | bytes 3686400 | tf_op jit(solution)/shard_map/all_gather | solution.py:31
  40.8 231.5 %all-gather.9.cloned.1.call-start = ((), (), s32[]{:S(2)}) async-start(), calls=%async_computation.6 | async-start | bytes 6553600 | tf_op jit(solution)/shard_map/all_gather | solution.py:27
  272.3 11.2 %copy-start.3 = (bf16[32,160,64]{1,2,0:T(8,128)(2,1)S(1)}, bf16[32,160,64]{1,2,0:T(8,128)(2,1)}, u32[]{:S(2)}) copy-start(bf16[32,160,64]{1,2,0:T(8,128)(2,1)} %param.10) | copy-start | bytes 1966084
  286.2 2.6 copy-start.2
  288.8 18.8 %all-to-all-start.2 = ((bf16[32,160,64]{1,2,0:T(8,128)(2,1)}), bf16[32,160,64]{1,2,0:T(8,128)(2,1)}, u32[]{:S(2)}, u32[]{:S(2)}) async-start(bf16[32,160,64]{1,2,0:T(8,128)(2,1)} %multiply_convert_fusion), calls=%async_computation.2 | async-start | bytes 2097152 | tf_op jit(solution)/shard_map/all_to_all | solution.py:138
  298.4 12.8 %copy-start.9 = (s32[168]{0:T(256)S(1)}, s32[168]{0:T(256)}, u32[]{:S(2)}) copy-start(s32[168]{0:T(256)} %param.19) | copy-start | bytes 2020
  298.4 13.1 %copy-start.5 = (bf16[160,640]{1,0:T(8,128)(2,1)S(1)}, bf16[160,640]{1,0:T(8,128)(2,1)}, u32[]{:S(2)}) copy-start(bf16[160,640]{1,0:T(8,128)(2,1)} %param.15) | copy-start | bytes 614404
  307.6 54.4 %all-to-all-start.1 = ((bf16[32,320,128]{2,1,0:T(8,128)(2,1)}), bf16[32,320,128]{2,1,0:T(8,128)(2,1)S(1)}, u32[]{:S(2)}, u32[]{:S(2)}) async-start(bf16[32,320,128]{2,1,0:T(8,128)(2,1)} %broadcast_select_fusion), calls=%async_computation.1 | async-start | bytes 5242880 | tf_op jit(solution)/shard_map/all_to_all | solution.py:139
  362.2 1.7 copy-start.4
  397.2 7.1 %copy-start.1 = (bf16[42,320,128]{2,1,0:T(8,128)(2,1)S(1)}, bf16[42,320,128]{2,1,0:T(8,128)(2,1)}, u32[]{:S(2)}) copy-start(bf16[42,320,128]{2,1,0:T(8,128)(2,1)} %param.14) | copy-start | bytes 10321924
Sparse Core Ops, SparseCore 0:
  8.9 104.5 all-gather.6
  115.1 38.4 all-gather.4
  155.2 76.6 all-gather.10
  233.3 38.9 all-gather.8
where the time goes:
time: 412 us; the launch traced here: 411 us
  waiting for transfers between devices  224 us (54%)
  blocking collectives  52.4 us (13%)
  matrix products  41.2 us (10%)
  local copies, waits for them, and re-layouts  36.7 us (9%)
  other arithmetic  28.6 us (7%)
  starting transfers between devices  14.4 us (3%)
  between operations  13.6 us (3%)
    all_gather x2, waiting for transfers between devices, gather_kernel(): return lax.all_gather(weight_shard, 'dp', axis=0, tiled=True)  133 us
    all_gather x2, waiting for transfers between devices, gather_channels(): return lax.all_gather(field, 'mp', axis=1, tiled=True)  80.5 us
    all_gather x2, blocking collectives, gather_projection(): return lax.all_gather(weight_shard, 'dp', axis=0, tiled=True)  39.2 us
    dot_general x2, matrix products, apply_kernel(): jnp.einsum('scq,cte->steq', full_field, kernel, preferred_element_type=jn...  22.4 us
    all_to_all x1, blocking collectives, local(): lax.all_to_all(attended, 'mp', split_axis=1, concat_axis=0, tiled=True)  13.2 us
    dot_general x1, matrix products, local(): jnp.einsum('shqk,shdk->shdq', attention, value_heads, preferred_element_t...  11.1 us
    all_to_all x1, waiting for transfers between devices, local(): lax.all_to_all(normed_out, 'mp', split_axis=0, concat_axis=1, tiled=True)  9.13 us
  transfers between devices with their start and end apart: 7, of which 5 were waited for; matrix products, arithmetic and copies ran while one was open for 18% of the time, Pallas kernels for 0%

commit v1 on v0

--- a/solution.py
+++ b/solution.py
@@ -25,6 +25,27 @@
 
 def gather_channels(field):
     return lax.all_gather(field, "mp", axis=1, tiled=True)
+
+
+def pair_gather_channels(field):
+    across = lax.ppermute(field, "mp", [(i, i ^ 2) for i in range(4)])
+    beside = lax.ppermute(field, "mp", [(i, i ^ 1) for i in range(4)])
+    relayed = lax.ppermute(across, "mp", [(i, i ^ 1) for i in range(4)])
+    return jnp.concatenate([field, beside, across, relayed], axis=1)
+
+
+def shift_parts(shard, count):
+    parts = [shard]
+    for step in range(1, count):
+        parts.append(lax.ppermute(shard, "dp", [(i, (i + step) % count) for i in range(count)]))
+    return jnp.stack(parts)
+
+
+def order_rows(stacked, wanted_blocks):
+    my_shard = lax.axis_index("dp")
+    count = stacked.shape[0]
+    picked = jnp.take(stacked, (my_shard - wanted_blocks) % count, axis=0, mode="clip")
+    return picked.reshape((count * stacked.shape[1],) + stacked.shape[2:])
 
 
 def gather_kernel(weight_shard):
@@ -110,16 +131,35 @@
     )
     prompt_hits = prompt_ids[:, None] == jnp.arange(lengths.shape[0], dtype=jnp.int32)[None, :]
     my_lengths = jnp.sum(jnp.where(prompt_hits, lengths[None, :], 0), axis=1)
+    fast = dp_count == 4 and mp_count == 4
+    weight_shards = (first_kernel, second_kernel, query_weight, output_weight)
+    if fast:
+        block_ids = jnp.arange(dp_count, dtype=jnp.int32)
+        channel_blocks = jnp.bitwise_xor(block_ids, my_column)
+        full_weights = (
+            order_rows(shift_parts(first_kernel, dp_count), channel_blocks),
+            order_rows(shift_parts(second_kernel, dp_count), channel_blocks),
+            order_rows(shift_parts(query_weight, dp_count), block_ids),
+            order_rows(shift_parts(output_weight, dp_count), block_ids),
+        )
+        spread_channels = pair_gather_channels
+    else:
+        full_weights = (
+            gather_kernel(first_kernel),
+            gather_kernel(second_kernel),
+            gather_projection(query_weight),
+            gather_projection(output_weight),
+        )
+        spread_channels = gather_channels
     start_field = latents.astype(jnp.float32)
     activated = jax.nn.silu(norm_groups(start_field, group_width)).astype(jnp.bfloat16)
-    first_in = gather_channels(activated)
-    weight_shards = (first_kernel, second_kernel, query_weight, output_weight)
+    first_in = spread_channels(activated)
 
     def convolve(full_field, which_weight):
-        return apply_kernel(full_field, gather_kernel(weight_shards[which_weight]))
+        return apply_kernel(full_field, full_weights[which_weight])
 
     def project(field_rows, which_weight):
-        full_weight = gather_projection(weight_shards[which_weight])
+        full_weight = full_weights[which_weight]
         return jnp.einsum(
             "scq,ce->seq", field_rows, full_weight, preferred_element_type=jnp.float32
         )
@@ -130,7 +170,7 @@
     modulated = jax.nn.silu(
         norm_groups(first_out, group_width) * (1.0 + scale_term) + shift_term
     ).astype(jnp.bfloat16)
-    second_in = gather_channels(modulated)
+    second_in = spread_channels(modulated)
     residual = start_field + convolve(second_in, 1)
     normed_out = norm_groups(residual, group_width).astype(jnp.bfloat16)
     local_samples = sample_shard_count // mp_count

time: 412 us -> 436 us (1.058)
  starting transfers between devices: 14.4 us -> 64.5 us
  blocking collectives: 52.4 us -> 13 us
  local copies, waits for them, and re-layouts: 36.7 us -> 51.9 us
  between operations: 13.6 us -> 0.65 us
  waiting for transfers between devices: 224 us -> 230 us
    ppermute x0 -> x18, waiting for transfers between devices: none -> 220 us  [the longest x12 199 us: shift_parts(): lax.ppermute(shard, 'dp', [(i, (i + step) % count) for i in range(count)])]
    all_gather x4 -> x0, waiting for transfers between devices: 213 us -> none  [the longest x2 133 us: gather_kernel(): return lax.all_gather(weight_shard, 'dp', axis=0, tiled=True)]
    ppermute x0 -> x18, starting transfers between devices: none -> 50.2 us  [the longest x12 46.8 us: shift_parts(): lax.ppermute(shard, 'dp', [(i, (i + step) % count) for i in range(count)])]
    all_gather x2 -> x0, blocking collectives: 39.2 us -> none  [gather_projection(): return lax.all_gather(weight_shard, 'dp', axis=0, tiled=True)]
    gather x0 -> x6, local copies, waits for them, and re-layouts: none -> 20.6 us  [order_rows(): jnp.take(stacked, (my_shard - wanted_blocks) % count, axis=0, mode='clip')]
    another operation x2 -> x6, other arithmetic: 0.18 us -> 8.11 us  [the longest x4 7.93 us: shift_parts(): return jnp.stack(parts)]
    reshape x0 -> x3, local copies, waits for them, and re-layouts: none -> 6.55 us  [the longest x2 5.92 us: order_rows(): return picked.reshape((count * stacked.shape[1],) + stacked.shape[2:])]
    all_to_all x2 -> x0, local copies, waits for them, and re-layouts: 5.95 us -> none  [local(): lax.all_to_all(normed_out, 'mp', split_axis=0, concat_axis=1, tiled=True)]
  transfers between devices with their start and end apart: 7 -> 21, of which waited for: 5 -> 11; matrix products, arithmetic and copies ran while one was open for 18% -> 19% of each run, Pallas kernels for 0% -> 0%
where the time goes in v1:
time: 436 us; the launch traced here: 434 us
  waiting for transfers between devices  230 us (53%)
  starting transfers between devices  64.5 us (15%)
  local copies, waits for them, and re-layouts  51.9 us (12%)
  matrix products  41.8 us (10%)
  other arithmetic  32.2 us (7%)
  blocking collectives  13 us (3%)
    ppermute x12, waiting for transfers between devices, shift_parts(): lax.ppermute(shard, 'dp', [(i, (i + step) % count) for i in range(count)])  199 us
    ppermute x12, starting transfers between devices, shift_parts(): lax.ppermute(shard, 'dp', [(i, (i + step) % count) for i in range(count)])  46.8 us
    dot_general x2, matrix products, apply_kernel(): jnp.einsum('scq,cte->steq', full_field, kernel, preferred_element_type=jn...  22.8 us
    ppermute x2, waiting for transfers between devices, pair_gather_channels(): across = lax.ppermute(field, 'mp', [(i, i ^ 2) for i in range(4)])  21.7 us
    gather x6, local copies, waits for them, and re-layouts, order_rows(): jnp.take(stacked, (my_shard - wanted_blocks) % count, axis=0, mode='clip')  20.6 us
    all_to_all x1, blocking collectives, local(): lax.all_to_all(attended, 'mp', split_axis=1, concat_axis=0, tiled=True)  13 us
    dot_general x1, matrix products, local(): jnp.einsum('shqk,shdk->shdq', attention, value_heads, preferred_element_t...  11.1 us
    all_to_all x1, waiting for transfers between devices, local(): lax.all_to_all(normed_out, 'mp', split_axis=0, concat_axis=1, tiled=True)  9.13 us
  transfers between devices with their start and end apart: 21, of which 11 were waited for; matrix products, arithmetic and copies ran while one was open for 19% of the time, Pallas kernels for 0%

profile of v1, /device:TPU:0, one launch (start us, length us, event | category | flops | bytes accessed | tf_op | source)
XLA Modules:
  0.0 433.6 jit_solution(7232761819546583479)
XLA Ops:
  2.3 3.5 gather_fusion.3
  5.8 5.5 %select_select_fusion = bf16[4,16,320,128]{3,2,1,0:T(8,128)(2,1)} fusion(bf16[4,16,320,128]{3,2,1,0:T(8,128)(2,1)} %bitcast.138, pred[4,16]{1,0:T(4,128)(4,1)S(1)} %compare_and_fusion, pred[4,16]{1,0:T(4,128)(4,1)S(1)} %broadcast_in_dim.133), kind=kLoop, calls=%fused_computation.25 | loop fusion | flops 5242880 | bytes 10485888 | tf_op jit(solution)/shard_map/jit(_where)/select_n | solution.py:117
  11.3 6.4 %all-to-all-start = ((bf16[4,16,320,128]{3,2,1,0:T(8,128)(2,1)}), bf16[4,16,320,128]{3,2,1,0:T(8,128)(2,1)}, u32[]{:S(2)}, u32[]{:S(2)}) async-start(bf16[4,16,320,128]{3,2,1,0:T(8,128)(2,1)} %select_select_fusion), calls=%async_computation | async-start | bytes 10485760 | tf_op jit(solution)/shard_map/all_to_all | solution.py:119
  28.5 17.6 %collective-permute-done.7 = bf16[32,160,64]{1,2,0:T(8,128)(2,1)} collective-permute-done((bf16[32,160,64]{1,2,0:T(8,128)(2,1)}, bf16[32,160,64]{1,2,0:T(8,128)(2,1)}, u32[]{:S(2)}, u32[]{:S(2)}) %collective-permute-start.7) | collective-permute-done | bytes 655392 | tf_op jit(solution)/shard_map/ppermute | solution.py:31
  46.1 77.5 %collective-permute-done.3 = bf16[160,9,160]{2,0,1:T(8,128)(2,1)S(1)} collective-permute-done((bf16[160,9,160]{2,0,1:T(8,128)(2,1)S(1)}, bf16[160,9,160]{2,0,1:T(8,128)(2,1)S(1)}, u32[]{:S(2)}, u32[]{:S(2)}) %collective-permute-start.3) | collective-permute-done | bytes 460832 | tf_op jit(solution)/shard_map/ppermute | solution.py:40
  123.6 58.6 %collective-permute-done.4 = bf16[160,9,160]{2,0,1:T(8,128)(2,1)S(1)} collective-permute-done((bf16[160,9,160]{2,0,1:T(8,128)(2,1)S(1)}, bf16[160,9,160]{2,0,1:T(8,128)(2,1)S(1)}, u32[]{:S(2)}, u32[]{:S(2)}) %collective-permute-start.4) | collective-permute-done | bytes 460832 | tf_op jit(solution)/shard_map/ppermute | solution.py:40
  185.5 2.4 gather_fusion.1
  187.9 6.2 %copy.50 = bf16[4,160,9,160]{1,0,3,2:T(4,128)(2,1)S(1)} copy(bf16[4,160,9,160]{3,1,2,0:T(8,128)(2,1)} %gather_fusion.1) | data formatting | bytes 3686400 | tf_op jit(solution)/shard_map/jit(_take)/gather | solution.py:47
  194.1 3.0 reshape.482
  197.1 11.4 %convolution_bitcast_fusion.1 = f32[32,9,160,8,8]{2,4,3,0,1:T(8,128)S(1)} fusion(bf16[32,160,64]{1,2,0:T(8,128)(2,1)} %collective-permute-done.8, bf16[32,160,64]{1,2,0:T(8,128)(2,1)} %collective-permute-done.7, bf16[32,160,64]{1,2,0:T(8,128)(2,1)} %collective-permute-done.6, bf16[32,160,64]{1,2,0:T(8,128)(2,1)} %fusion.36, ...), kind=kOutput, calls=%fused_computation.24 | convolution fusion | flops 3785359360 | bytes 16261120 | tf_op jit(solution)/shard_map/scq,cte->steq/dot_general | solution.py:62
  215.4 15.0 %collective-permute-start = (bf16[160,9,160]{2,0,1:T(8,128)(2,1)S(1)}, bf16[160,9,160]{2,0,1:T(8,128)(2,1)S(1)}, u32[]{:S(2)}, u32[]{:S(2)}) collective-permute-start(bf16[160,9,160]{2,0,1:T(8,128)(2,1)S(1)} %copy-done.7), channel_id=1, source_target_pairs={{0,4},{4,8},{8,12},{12,0},{1,5},{5,9},{9,13},{13,1},{2,6},{6,10},{... | collective-permute-start | bytes 1382408 | tf_op jit(solution)/shard_map/ppermute | solution.py:40
  233.1 4.1 collective-permute-done.10
  237.6 11.5 %collective-permute-done = bf16[160,9,160]{2,0,1:T(8,128)(2,1)S(1)} collective-permute-done((bf16[160,9,160]{2,0,1:T(8,128)(2,1)S(1)}, bf16[160,9,160]{2,0,1:T(8,128)(2,1)S(1)}, u32[]{:S(2)}, u32[]{:S(2)}) %collective-permute-start) | collective-permute-done | bytes 460832 | tf_op jit(solution)/shard_map/ppermute | solution.py:40
  249.1 29.5 %collective-permute-done.1 = bf16[160,9,160]{2,0,1:T(8,128)(2,1)S(1)} collective-permute-done((bf16[160,9,160]{2,0,1:T(8,128)(2,1)S(1)}, bf16[160,9,160]{2,0,1:T(8,128)(2,1)S(1)}, u32[]{:S(2)}, u32[]{:S(2)}) %collective-permute-start.1) | collective-permute-done | bytes 460832 | tf_op jit(solution)/shard_map/ppermute | solution.py:40
  281.6 2.4 gather_fusion
  284.1 6.2 %copy.49 = bf16[4,160,9,160]{1,0,3,2:T(4,128)(2,1)S(1)} copy(bf16[4,160,9,160]{3,1,2,0:T(8,128)(2,1)} %gather_fusion) | data formatting | bytes 3686400 | tf_op jit(solution)/shard_map/jit(_take)/gather | solution.py:47
  290.3 3.0 reshape.484
  293.2 11.5 %convolution_bitcast_fusion = f32[32,9,160,8,8]{2,4,3,0,1:T(8,128)S(1)} fusion(bf16[32,160,64]{1,2,0:T(8,128)(2,1)} %collective-permute-done.11, bf16[32,160,64]{1,2,0:T(8,128)(2,1)} %collective-permute-done.10, bf16[32,160,64]{1,2,0:T(8,128)(2,1)} %collective-permute-done.9, bf16[32,160,64]{1,2,0:T(8,128)(2,1)} %multiply_convert_fusion.1, ...), kind=kOutput, calls=%fused_computation.23 | convolution fusion | flops 3785359360 | bytes 16261120 | tf_op jit(solution)/shard_map/scq,cte->steq/dot_general | solution.py:62
  304.7 2.4 fusion.74
  309.7 4.3 all-to-all-start.2
  314.0 3.5 gather_fusion.4
  319.4 9.1 %all-to-all-done.2 = bf16[32,160,64]{1,2,0:T(8,128)(2,1)} async-done(((bf16[32,160,64]{1,2,0:T(8,128)(2,1)}), bf16[32,160,64]{1,2,0:T(8,128)(2,1)}, u32[]{:S(2)}, u32[]{:S(2)}) %all-to-all-start.2) | async-done | bytes 655392 | tf_op jit(solution)/shard_map/all_to_all | solution.py:178
  328.5 3.7 all-to-all-start.1
  332.2 15.6 %collective-permute-start.15 = (bf16[160,640]{1,0:T(8,128)(2,1)S(1)}, bf16[160,640]{1,0:T(8,128)(2,1)S(1)}, u32[]{:S(2)}, u32[]{:S(2)}) collective-permute-start(bf16[160,640]{1,0:T(8,128)(2,1)S(1)} %copy-done.13), channel_id=1, source_target_pairs={{0,4},{4,8},{8,12},{12,0},{1,5},{5,9},{9,13},{13,1},{2,6},{6,10},{... | collective-permute-start | bytes 614408 | tf_op jit(solution)/shard_map/ppermute | solution.py:40
  355.2 3.1 collective-permute-start.14
  358.4 5.7 %collective-permute-done.16 = bf16[160,640]{1,0:T(8,128)(2,1)S(1)} collective-permute-done((bf16[160,640]{1,0:T(8,128)(2,1)S(1)}, bf16[160,640]{1,0:T(8,128)(2,1)S(1)}, u32[]{:S(2)}, u32[]{:S(2)}) %collective-permute-start.16) | collective-permute-done | bytes 204832 | tf_op jit(solution)/shard_map/ppermute | solution.py:40
  368.6 12.9 %collective-permute-done.13 = bf16[160,640]{1,0:T(8,128)(2,1)} collective-permute-done((bf16[160,640]{1,0:T(8,128)(2,1)}, bf16[160,640]{1,0:T(8,128)(2,1)}, u32[]{:S(2)}, u32[]{:S(2)}) %collective-permute-start.13) | collective-permute-done | bytes 204832 | tf_op jit(solution)/shard_map/ppermute | solution.py:40
  385.5 3.1 fusion.50
  396.9 11.1 %convolution_convert_fusion = bf16[8,10,64,64]{3,2,1,0:T(8,128)(2,1)S(1)} fusion(bf16[8,10,64,128]{3,2,1,0:T(8,128)(2,1)} %bitcast.150, f32[8,10,64]{2,1,0:T(8,128)S(1)} %fusion.79, f32[8,10,64,128]{3,2,1,0:T(8,128)} %fusion.80, pred[8,128]{1,0:T(8,128)(4,1)S(1)} %iota_compare_fusion.4), kind=kOutput, calls=%fused_computation.87 | convolution fusion | flops 87495808 | bytes 4609024 | tf_op jit(solution)/shard_map/shqk,shdk->shdq/dot_general | solution.py:201
  411.8 13.0 %all_to_all.47 = bf16[4,2,40960]{2,1,0:T(2,128)(2,1)S(1)} all-to-all(bf16[4,2,40960]{2,1,0:T(2,128)(2,1)S(1)} %reshape.493), channel_id=1, replica_groups=mesh['groups'=2,'dp'=4,'mp'=4] {'mp'}, dimensions={0} | all-to-all | bytes 1310720 | tf_op jit(solution)/shard_map/all_to_all | solution.py:207
  426.6 3.5 copy.60
  430.1 3.5 fusion.38
  (156 shorter events, 63.1 us)
Async XLA Ops:
  11.3 6.5 %copy-start.3 = (bf16[32,160,64]{1,2,0:T(8,128)(2,1)S(1)}, bf16[32,160,64]{1,2,0:T(8,128)(2,1)}, u32[]{:S(2)}) copy-start(bf16[32,160,64]{1,2,0:T(8,128)(2,1)} %param.10) | copy-start | bytes 1966084
  11.3 298.4 %all-to-all-start = ((bf16[4,16,320,128]{3,2,1,0:T(8,128)(2,1)}), bf16[4,16,320,128]{3,2,1,0:T(8,128)(2,1)}, u32[]{:S(2)}, u32[]{:S(2)}) async-start(bf16[4,16,320,128]{3,2,1,0:T(8,128)(2,1)} %select_select_fusion), calls=%async_computation | async-start | bytes 10485760 | tf_op jit(solution)/shard_map/all_to_all | solution.py:119
  18.3 10.1 %copy-start.17 = (bf16[32,2,160]{2,1,0:T(2,128)(2,1)S(1)}, bf16[32,2,160]{2,1,0:T(2,128)(2,1)}, u32[]{:S(2)}) copy-start(bf16[32,2,160]{2,1,0:T(2,128)(2,1)} %param.11) | copy-start | bytes 61444
  20.9 25.1 %collective-permute-start.7 = (bf16[32,160,64]{1,2,0:T(8,128)(2,1)}, bf16[32,160,64]{1,2,0:T(8,128)(2,1)}, u32[]{:S(2)}, u32[]{:S(2)}) collective-permute-start(bf16[32,160,64]{1,2,0:T(8,128)(2,1)} %fusion.36), channel_id=1, source_target_pairs={{0,2},{1,3},{2,0},{3,1},{4,6},{5,7},{6,4},{7,5},{8,10},{9,11},{10,... | collective-permute-start | bytes 1966088 | tf_op jit(solution)/shard_map/ppermute | solution.py:31
  22.6 101.0 %collective-permute-start.3 = (bf16[160,9,160]{2,0,1:T(8,128)(2,1)S(1)}, bf16[160,9,160]{2,0,1:T(8,128)(2,1)S(1)}, u32[]{:S(2)}, u32[]{:S(2)}) collective-permute-start(bf16[160,9,160]{2,0,1:T(8,128)(2,1)S(1)} %copy-done.6), channel_id=1, source_target_pairs={{0,4},{4,8},{8,12},{12,0},{1,5},{5,9},{9,13},{13,1},{2,6},{6,10},{... | collective-permute-start | bytes 1382408 | tf_op jit(solution)/shard_map/ppermute | solution.py:40
  24.6 157.7 %collective-permute-start.4 = (bf16[160,9,160]{2,0,1:T(8,128)(2,1)S(1)}, bf16[160,9,160]{2,0,1:T(8,128)(2,1)S(1)}, u32[]{:S(2)}, u32[]{:S(2)}) collective-permute-start(bf16[160,9,160]{2,0,1:T(8,128)(2,1)S(1)} %copy-done.6), channel_id=1, source_target_pairs={{0,8},{4,12},{8,0},{12,4},{1,9},{5,13},{9,1},{13,5},{2,10},{6,14},... | collective-permute-start | bytes 1382408 | tf_op jit(solution)/shard_map/ppermute | solution.py:40
  26.9 155.3 %collective-permute-start.5 = (bf16[160,9,160]{2,0,1:T(8,128)(2,1)S(1)}, bf16[160,9,160]{2,0,1:T(8,128)(2,1)S(1)}, u32[]{:S(2)}, u32[]{:S(2)}) collective-permute-start(bf16[160,9,160]{2,0,1:T(8,128)(2,1)S(1)} %copy-done.6), channel_id=1, source_target_pairs={{0,12},{4,0},{8,4},{12,8},{1,13},{5,1},{9,5},{13,9},{2,14},{6,2},{... | collective-permute-start | bytes 1382408 | tf_op jit(solution)/shard_map/ppermute | solution.py:40
  28.4 168.7 %collective-permute-start.6 = (bf16[32,160,64]{1,2,0:T(8,128)(2,1)}, bf16[32,160,64]{1,2,0:T(8,128)(2,1)}, u32[]{:S(2)}, u32[]{:S(2)}) collective-permute-start(bf16[32,160,64]{1,2,0:T(8,128)(2,1)} %fusion.36), channel_id=1, source_target_pairs={{0,1},{1,0},{2,3},{3,2},{4,5},{5,4},{6,7},{7,6},{8,9},{9,8},{10,11... | collective-permute-start | bytes 1966088 | tf_op jit(solution)/shard_map/ppermute | solution.py:32
  46.1 151.0 %collective-permute-start.8 = (bf16[32,160,64]{1,2,0:T(8,128)(2,1)}, bf16[32,160,64]{1,2,0:T(8,128)(2,1)}, u32[]{:S(2)}, u32[]{:S(2)}) collective-permute-start(bf16[32,160,64]{1,2,0:T(8,128)(2,1)} %collective-permute-done.7), channel_id=1, source_target_pairs={{0,1},{1,0},{2,3},{3,2},{4,5},{5,4},{6,7},{7,6},{8,9},{9,8},{10,11... | collective-permute-start | bytes 1966088 | tf_op jit(solution)/shard_map/ppermute | solution.py:33
  123.6 58.7 %copy-start.10 = (bf16[160,9,160]{2,0,1:T(8,128)(2,1)}, bf16[160,9,160]{2,0,1:T(8,128)(2,1)S(1)}, u32[]{:S(2)}) copy-start(bf16[160,9,160]{2,0,1:T(8,128)(2,1)S(1)} %collective-permute-done.3) | copy-start | bytes 1382404
  211.6 21.2 %copy-start.18 = (s32[128]{0:T(128)S(1)}, s32[128]{0:T(128)}, u32[]{:S(2)}) copy-start(s32[128]{0:T(128)} %param.18) | copy-start | bytes 1540
  211.6 25.9 %copy-start.19 = (s32[128]{0:T(128)S(1)}, s32[128]{0:T(128)}, u32[]{:S(2)}) copy-start(s32[128]{0:T(128)} %param.17) | copy-start | bytes 1540
  213.8 23.5 %collective-permute-start.10 = (bf16[32,160,64]{1,2,0:T(8,128)(2,1)}, bf16[32,160,64]{1,2,0:T(8,128)(2,1)}, u32[]{:S(2)}, u32[]{:S(2)}) collective-permute-start(bf16[32,160,64]{1,2,0:T(8,128)(2,1)} %multiply_convert_fusion.1), channel_id=1, source_target_pairs={{0,2},{1,3},{2,0},{3,1},{4,6},{5,7},{6,4},{7,5},{8,10},{9,11},{10,... | collective-permute-start | bytes 1966088 | tf_op jit(solution)/shard_map/ppermute | solution.py:31
  215.4 33.7 %collective-permute-start = (bf16[160,9,160]{2,0,1:T(8,128)(2,1)S(1)}, bf16[160,9,160]{2,0,1:T(8,128)(2,1)S(1)}, u32[]{:S(2)}, u32[]{:S(2)}) collective-permute-start(bf16[160,9,160]{2,0,1:T(8,128)(2,1)S(1)} %copy-done.7), channel_id=1, source_target_pairs={{0,4},{4,8},{8,12},{12,0},{1,5},{5,9},{9,13},{13,1},{2,6},{6,10},{... | collective-permute-start | bytes 1382408 | tf_op jit(solution)/shard_map/ppermute | solution.py:40
  230.4 48.2 %collective-permute-start.1 = (bf16[160,9,160]{2,0,1:T(8,128)(2,1)S(1)}, bf16[160,9,160]{2,0,1:T(8,128)(2,1)S(1)}, u32[]{:S(2)}, u32[]{:S(2)}) collective-permute-start(bf16[160,9,160]{2,0,1:T(8,128)(2,1)S(1)} %copy-done.7), channel_id=1, source_target_pairs={{0,8},{4,12},{8,0},{12,4},{1,9},{5,13},{9,1},{13,5},{2,10},{6,14},... | collective-permute-start | bytes 1382408 | tf_op jit(solution)/shard_map/ppermute | solution.py:40
  232.1 46.5 %collective-permute-start.2 = (bf16[160,9,160]{2,0,1:T(8,128)(2,1)S(1)}, bf16[160,9,160]{2,0,1:T(8,128)(2,1)}, u32[]{:S(2)}, u32[]{:S(2)}) collective-permute-start(bf16[160,9,160]{2,0,1:T(8,128)(2,1)S(1)} %copy-done.7), channel_id=1, source_target_pairs={{0,12},{4,0},{8,4},{12,8},{1,13},{5,1},{9,5},{13,9},{2,14},{6,2},{... | collective-permute-start | bytes 1382408 | tf_op jit(solution)/shard_map/ppermute | solution.py:40
  233.1 60.2 %collective-permute-start.9 = (bf16[32,160,64]{1,2,0:T(8,128)(2,1)}, bf16[32,160,64]{1,2,0:T(8,128)(2,1)}, u32[]{:S(2)}, u32[]{:S(2)}) collective-permute-start(bf16[32,160,64]{1,2,0:T(8,128)(2,1)} %multiply_convert_fusion.1), channel_id=1, source_target_pairs={{0,1},{1,0},{2,3},{3,2},{4,5},{5,4},{6,7},{7,6},{8,9},{9,8},{10,11... | collective-permute-start | bytes 1966088 | tf_op jit(solution)/shard_map/ppermute | solution.py:32
  237.2 56.0 %collective-permute-start.11 = (bf16[32,160,64]{1,2,0:T(8,128)(2,1)}, bf16[32,160,64]{1,2,0:T(8,128)(2,1)}, u32[]{:S(2)}, u32[]{:S(2)}) collective-permute-start(bf16[32,160,64]{1,2,0:T(8,128)(2,1)} %collective-permute-done.10), channel_id=1, source_target_pairs={{0,1},{1,0},{2,3},{3,2},{4,5},{5,4},{6,7},{7,6},{8,9},{9,8},{10,11... | collective-permute-start | bytes 1966088 | tf_op jit(solution)/shard_map/ppermute | solution.py:33
  249.1 29.5 %copy-start.8 = (bf16[160,9,160]{2,0,1:T(8,128)(2,1)}, bf16[160,9,160]{2,0,1:T(8,128)(2,1)S(1)}, u32[]{:S(2)}) copy-start(bf16[160,9,160]{2,0,1:T(8,128)(2,1)S(1)} %collective-permute-done) | copy-start | bytes 1382404
  293.2 11.5 %copy-start.4 = (bf16[32,160,64]{1,2,0:T(8,128)(2,1)S(1)}, bf16[32,160,64]{1,2,0:T(8,128)(2,1)}, u32[]{:S(2)}) copy-start(bf16[32,160,64]{1,2,0:T(8,128)(2,1)} %param.10) | copy-start | bytes 1966084
  309.7 18.8 %all-to-all-start.2 = ((bf16[32,160,64]{1,2,0:T(8,128)(2,1)}), bf16[32,160,64]{1,2,0:T(8,128)(2,1)}, u32[]{:S(2)}, u32[]{:S(2)}) async-start(bf16[32,160,64]{1,2,0:T(8,128)(2,1)} %multiply_convert_fusion), calls=%async_computation.2 | async-start | bytes 2097152 | tf_op jit(solution)/shard_map/all_to_all | solution.py:178
  319.4 12.8 %copy-start.13 = (bf16[160,640]{1,0:T(8,128)(2,1)S(1)}, bf16[160,640]{1,0:T(8,128)(2,1)}, u32[]{:S(2)}) copy-start(bf16[160,640]{1,0:T(8,128)(2,1)} %param.15) | copy-start | bytes 614404
  319.4 33.3 %copy-start.20 = (s32[168]{0:T(256)S(1)}, s32[168]{0:T(256)}, u32[]{:S(2)}) copy-start(s32[168]{0:T(256)} %param.19) | copy-start | bytes 2020
  328.5 62.4 %all-to-all-start.1 = ((bf16[32,320,128]{2,1,0:T(8,128)(2,1)}), bf16[32,320,128]{2,1,0:T(8,128)(2,1)S(1)}, u32[]{:S(2)}, u32[]{:S(2)}) async-start(bf16[32,320,128]{2,1,0:T(8,128)(2,1)} %broadcast_select_fusion), calls=%async_computation.1 | async-start | bytes 5242880 | tf_op jit(solution)/shard_map/all_to_all | solution.py:179
  332.2 23.1 %collective-permute-start.15 = (bf16[160,640]{1,0:T(8,128)(2,1)S(1)}, bf16[160,640]{1,0:T(8,128)(2,1)S(1)}, u32[]{:S(2)}, u32[]{:S(2)}) collective-permute-start(bf16[160,640]{1,0:T(8,128)(2,1)S(1)} %copy-done.13), channel_id=1, source_target_pairs={{0,4},{4,8},{8,12},{12,0},{1,5},{5,9},{9,13},{13,1},{2,6},{6,10},{... | collective-permute-start | bytes 614408 | tf_op jit(solution)/shard_map/ppermute | solution.py:40
  347.8 16.3 %collective-permute-start.16 = (bf16[160,640]{1,0:T(8,128)(2,1)S(1)}, bf16[160,640]{1,0:T(8,128)(2,1)S(1)}, u32[]{:S(2)}, u32[]{:S(2)}) collective-permute-start(bf16[160,640]{1,0:T(8,128)(2,1)S(1)} %copy-done.13), channel_id=1, source_target_pairs={{0,8},{4,12},{8,0},{12,4},{1,9},{5,13},{9,1},{13,5},{2,10},{6,14},... | collective-permute-start | bytes 614408 | tf_op jit(solution)/shard_map/ppermute | solution.py:40
  349.7 14.3 %collective-permute-start.17 = (bf16[160,640]{1,0:T(8,128)(2,1)S(1)}, bf16[160,640]{1,0:T(8,128)(2,1)S(1)}, u32[]{:S(2)}, u32[]{:S(2)}) collective-permute-start(bf16[160,640]{1,0:T(8,128)(2,1)S(1)} %copy-done.13), channel_id=1, source_target_pairs={{0,12},{4,0},{8,4},{12,8},{1,13},{5,1},{9,5},{13,9},{2,14},{6,2},{... | collective-permute-start | bytes 614408 | tf_op jit(solution)/shard_map/ppermute | solution.py:40
  350.2 18.4 %collective-permute-start.12 = (bf16[160,640]{1,0:T(8,128)(2,1)}, bf16[160,640]{1,0:T(8,128)(2,1)}, u32[]{:S(2)}, u32[]{:S(2)}) collective-permute-start(bf16[160,640]{1,0:T(8,128)(2,1)} %param.16), channel_id=1, source_target_pairs={{0,4},{4,8},{8,12},{12,0},{1,5},{5,9},{9,13},{13,1},{2,6},{6,10},{... | collective-permute-start | bytes 614408 | tf_op jit(solution)/shard_map/ppermute | solution.py:40
  351.8 29.7 %collective-permute-start.13 = (bf16[160,640]{1,0:T(8,128)(2,1)}, bf16[160,640]{1,0:T(8,128)(2,1)}, u32[]{:S(2)}, u32[]{:S(2)}) collective-permute-start(bf16[160,640]{1,0:T(8,128)(2,1)} %param.16), channel_id=1, source_target_pairs={{0,8},{4,12},{8,0},{12,4},{1,9},{5,13},{9,1},{13,5},{2,10},{6,14},... | collective-permute-start | bytes 614408 | tf_op jit(solution)/shard_map/ppermute | solution.py:40
  355.2 8.8 %copy-start.14 = (bf16[160,640]{1,0:T(8,128)(2,1)}, bf16[160,640]{1,0:T(8,128)(2,1)S(1)}, u32[]{:S(2)}) copy-start(bf16[160,640]{1,0:T(8,128)(2,1)S(1)} %collective-permute-done.15) | copy-start | bytes 614404
  355.2 26.2 %collective-permute-start.14 = (bf16[160,640]{1,0:T(8,128)(2,1)}, bf16[160,640]{1,0:T(8,128)(2,1)}, u32[]{:S(2)}, u32[]{:S(2)}) collective-permute-start(bf16[160,640]{1,0:T(8,128)(2,1)} %param.16), channel_id=1, source_target_pairs={{0,12},{4,0},{8,4},{12,8},{1,13},{5,1},{9,5},{13,9},{2,14},{6,2},{... | collective-permute-start | bytes 614408 | tf_op jit(solution)/shard_map/ppermute | solution.py:40
  426.6 7.1 %copy-start.1 = (bf16[42,320,128]{2,1,0:T(8,128)(2,1)S(1)}, bf16[42,320,128]{2,1,0:T(8,128)(2,1)}, u32[]{:S(2)}) copy-start(bf16[42,320,128]{2,1,0:T(8,128)(2,1)} %param.14) | copy-start | bytes 10321924
  (10 other events, 19.0 us)

commit v2 on v1

--- a/solution.py
+++ b/solution.py
@@ -32,6 +32,25 @@
     beside = lax.ppermute(field, "mp", [(i, i ^ 1) for i in range(4)])
     relayed = lax.ppermute(across, "mp", [(i, i ^ 1) for i in range(4)])
     return jnp.concatenate([field, beside, across, relayed], axis=1)
+
+
+def line_gather_flat(flat, count):
+    my_shard = lax.axis_index("dp")
+    rightward = [(i, i + 1) for i in range(count - 1)]
+    leftward = [(i + 1, i) for i in range(count - 1)]
+    going_right, going_left = flat, flat
+    held = [flat]
+    from_left, from_right = [], []
+    for _ in range(1, count):
+        going_right = lax.ppermute(going_right, "dp", rightward)
+        going_left = lax.ppermute(going_left, "dp", leftward)
+        from_left.append(going_right)
+        from_right.append(going_left)
+    stacked = jnp.stack(held + from_left + from_right)
+    blocks = jnp.arange(count, dtype=jnp.int32)
+    gap = blocks - my_shard
+    slot = jnp.where(gap == 0, 0, jnp.where(gap < 0, -gap, count - 1 + gap))
+    return jnp.take(stacked, slot, axis=0, mode="clip")
 
 
 def shift_parts(shard, count):
@@ -116,7 +135,6 @@
     send_rows = jnp.take(encoder_cache, source_row, axis=0)
     send_rows = jnp.where(filled[:, None, None], send_rows, jnp.zeros_like(send_rows))
     outgoing = send_rows.reshape(dp_count, slot_limit, cache_width, cache_len)
-    incoming = lax.all_to_all(outgoing, "dp", split_axis=0, concat_axis=0, tiled=True)
     arriving = destination == my_shard
     arrival_pos = jnp.cumsum(arriving.astype(jnp.int32)) - 1
     selector = arriving[None, :] & (arrival_pos[None, :] == positions[:, None])
@@ -126,9 +144,6 @@
     incoming_order_rank = jnp.sum(jnp.where(selector, slot_rank.reshape(-1)[None, :], 0), axis=1)
     prompt_ids = jnp.sum(jnp.where(selector, kept_prompt_list[None, :], 0), axis=1)
     landing_slot = kept_prompt // sample_shard_count * slot_limit + incoming_order_rank
-    my_pairs = jnp.take(
-        incoming.reshape(dp_count * slot_limit, cache_width, cache_len), landing_slot, axis=0
-    )
     prompt_hits = prompt_ids[:, None] == jnp.arange(lengths.shape[0], dtype=jnp.int32)[None, :]
     my_lengths = jnp.sum(jnp.where(prompt_hits, lengths[None, :], 0), axis=1)
     fast = dp_count == 4 and mp_count == 4
@@ -136,12 +151,35 @@
     if fast:
         block_ids = jnp.arange(dp_count, dtype=jnp.int32)
         channel_blocks = jnp.bitwise_xor(block_ids, my_column)
-        full_weights = (
-            order_rows(shift_parts(first_kernel, dp_count), channel_blocks),
-            order_rows(shift_parts(second_kernel, dp_count), channel_blocks),
-            order_rows(shift_parts(query_weight, dp_count), block_ids),
-            order_rows(shift_parts(output_weight, dp_count), block_ids),
-        )
+        rows = first_kernel.shape[0]
+        lane = first_kernel.shape[2]
+        taps = first_kernel.shape[1]
+        packed = jnp.concatenate(
+            [
+                first_kernel,
+                second_kernel,
+                query_weight.reshape(rows, -1, lane),
+                output_weight.reshape(rows, -1, lane),
+            ],
+            axis=1,
+        )
+        gathered = line_gather_flat(packed, dp_count)
+        proj_taps = query_weight.shape[1] // lane
+        bounds = (
+            (0, taps, channel_blocks, None),
+            (taps, 2 * taps, channel_blocks, None),
+            (2 * taps, 2 * taps + proj_taps, block_ids, query_weight.shape[1]),
+            (2 * taps + proj_taps, 2 * taps + 2 * proj_taps, block_ids, output_weight.shape[1]),
+        )
+        full_weights = []
+        for low, high, order, width in bounds:
+            picked = jnp.take(gathered[:, :, low:high, :], order, axis=0, mode="clip")
+            if width is None:
+                full_weights.append(picked.reshape(dp_count * rows, high - low, lane))
+            else:
+                full_weights.append(picked.reshape(dp_count * rows, width))
+        full_weights = tuple(full_weights)
+        outgoing = lax.optimization_barrier((outgoing, gathered))[0]
         spread_channels = pair_gather_channels
     else:
         full_weights = (
@@ -151,6 +189,10 @@
             gather_projection(output_weight),
         )
         spread_channels = gather_channels
+    incoming = lax.all_to_all(outgoing, "dp", split_axis=0, concat_axis=0, tiled=True)
+    my_pairs = jnp.take(
+        incoming.reshape(dp_count * slot_limit, cache_width, cache_len), landing_slot, axis=0
+    )
     start_field = latents.astype(jnp.float32)
     activated = jax.nn.silu(norm_groups(start_field, group_width)).astype(jnp.bfloat16)
     first_in = spread_channels(activated)

time: 436 us -> 427 us (0.979); the launches traced: 434 us -> 420 us
  local copies, waits for them, and re-layouts: 51.9 us -> 130 us
  waiting for transfers between devices: 230 us -> 165 us
  starting transfers between devices: 64.5 us -> 36.9 us
    ppermute x12 -> x6, waiting for transfers between devices: 199 us -> 112 us  [the longest x3 104 us: line_gather_flat(): going_right = lax.ppermute(going_right, 'dp', rightward)]
    gather x6 -> x12, local copies, waits for them, and re-layouts: 20.6 us -> 48.5 us  [the longest x8 33 us: local(): picked = jnp.take(gathered[:, :, low:high, :], order, axis=0, mode='clip')]
    ppermute x12 -> x6, starting transfers between devices: 46.8 us -> 20.4 us  [the longest x3 16.5 us: line_gather_flat(): going_right = lax.ppermute(going_right, 'dp', rightward)]
    ppermute x2, waiting for transfers between devices: 21.7 us -> 44.7 us  [pair_gather_channels(): across = lax.ppermute(field, 'mp', [(i, i ^ 2) for i in range(4)])]
    unnamed x44 -> x37, local copies, waits for them, and re-layouts: 5.9 us -> 26 us
    reshape x2 -> x6, local copies, waits for them, and re-layouts: 5.92 us -> 17.5 us  [the longest x2 8.91 us: local(): full_weights.append(picked.reshape(dp_count * rows, high - low, lane))]
    slice x0 -> x2, local copies, waits for them, and re-layouts: none -> 8.22 us  [local(): picked = jnp.take(gathered[:, :, low:high, :], order, axis=0, mode='clip')]
    another operation x6 -> x2, other arithmetic: 8.11 us -> 0.18 us  [the longest x4 7.93 us: shift_parts(): return jnp.stack(parts)]
  transfers between devices with their start and end apart: 21 -> 15, of which waited for: 11 -> 7; matrix products, arithmetic and copies ran while one was open for 19% -> 32% of each run, Pallas kernels for 0% -> 0%
where the time goes in v2:
time: 427 us; the launch traced here: 420 us
  waiting for transfers between devices  165 us (39%)
  local copies, waits for them, and re-layouts  130 us (30%)
  matrix products  41 us (10%)
  starting transfers between devices  36.9 us (9%)
  other arithmetic  31.7 us (7%)
  blocking collectives  13.3 us (3%)
    ppermute x3, waiting for transfers between devices, line_gather_flat(): going_right = lax.ppermute(going_right, 'dp', rightward)  104 us
    ppermute x2, waiting for transfers between devices, pair_gather_channels(): across = lax.ppermute(field, 'mp', [(i, i ^ 2) for i in range(4)])  44.7 us
    gather x8, local copies, waits for them, and re-layouts, local(): picked = jnp.take(gathered[:, :, low:high, :], order, axis=0, mode='clip')  33 us
    unnamed x37, local copies, waits for them, and re-layouts  26 us
    dot_general x2, matrix products, apply_kernel(): jnp.einsum('scq,cte->steq', full_field, kernel, preferred_element_type=jn...  23 us
    ppermute x3, starting transfers between devices, line_gather_flat(): going_right = lax.ppermute(going_right, 'dp', rightward)  16.5 us
    gather x4, local copies, waits for them, and re-layouts, line_gather_flat(): return jnp.take(stacked, slot, axis=0, mode='clip')  15.6 us
    all_to_all x1, blocking collectives, local(): lax.all_to_all(attended, 'mp', split_axis=1, concat_axis=0, tiled=True)  13.3 us
  transfers between devices with their start and end apart: 15, of which 7 were waited for; matrix products, arithmetic and copies ran while one was open for 32% of the time, Pallas kernels for 0%

profile of v2, /device:TPU:0, one launch (start us, length us, event | category | flops | bytes accessed | tf_op | source)
XLA Modules:
  0.0 419.9 jit_solution(12804840726153638082)
XLA Ops:
  10.7 6.3 %collective-permute-start = (bf16[160,26,160]{2,0,1:T(8,128)(2,1)}, bf16[160,26,160]{2,0,1:T(8,128)(2,1)}, u32[]{:S(2)}, u32[]{:S(2)}) collective-permute-start(bf16[160,26,160]{2,0,1:T(8,128)(2,1)} %copy_dynamic-update-slice_fusion), channel_id=1, source_target_pairs={{0,4},{4,8},{8,12},{1,5},{5,9},{9,13},{2,6},{6,10},{10,14},{3,7},{... | collective-permute-start | bytes 3993608 | tf_op jit(solution)/shard_map/ppermute | solution.py:45
  27.6 33.9 %collective-permute-done = bf16[160,26,160]{2,0,1:T(8,128)(2,1)} collective-permute-done((bf16[160,26,160]{2,0,1:T(8,128)(2,1)}, bf16[160,26,160]{2,0,1:T(8,128)(2,1)}, u32[]{:S(2)}, u32[]{:S(2)}) %collective-permute-start) | collective-permute-done | bytes 1331232 | tf_op jit(solution)/shard_map/ppermute | solution.py:45
  61.5 5.7 %collective-permute-start.1 = (bf16[160,26,160]{2,0,1:T(8,128)(2,1)}, bf16[160,26,160]{2,0,1:T(8,128)(2,1)}, u32[]{:S(2)}, u32[]{:S(2)}) collective-permute-start(bf16[160,26,160]{2,0,1:T(8,128)(2,1)} %collective-permute-done), channel_id=1, source_target_pairs={{0,4},{4,8},{8,12},{1,5},{5,9},{9,13},{2,6},{6,10},{10,14},{3,7},{... | collective-permute-start | bytes 3993608 | tf_op jit(solution)/shard_map/ppermute | solution.py:45
  67.7 3.5 gather_fusion.3
  74.3 36.6 %collective-permute-done.1 = bf16[160,26,160]{2,0,1:T(8,128)(2,1)} collective-permute-done((bf16[160,26,160]{2,0,1:T(8,128)(2,1)}, bf16[160,26,160]{2,0,1:T(8,128)(2,1)}, u32[]{:S(2)}, u32[]{:S(2)}) %collective-permute-start.1) | collective-permute-done | bytes 1331232 | tf_op jit(solution)/shard_map/ppermute | solution.py:45
  110.9 4.5 %collective-permute-start.2 = (bf16[160,26,160]{2,0,1:T(8,128)(2,1)}, bf16[160,26,160]{2,0,1:T(8,128)(2,1)S(1)}, u32[]{:S(2)}, u32[]{:S(2)}) collective-permute-start(bf16[160,26,160]{2,0,1:T(8,128)(2,1)} %collective-permute-done.1), channel_id=1, source_target_pairs={{0,4},{4,8},{8,12},{1,5},{5,9},{9,13},{2,6},{6,10},{10,14},{3,7},{... | collective-permute-start | bytes 3993608 | tf_op jit(solution)/shard_map/ppermute | solution.py:45
  115.4 5.6 %select_select_fusion = bf16[4,16,320,128]{3,2,1,0:T(8,128)(2,1)} fusion(bf16[4,16,320,128]{3,2,1,0:T(8,128)(2,1)} %bitcast.132, pred[4,16]{1,0:T(4,128)(4,1)S(1)} %compare_and_fusion, pred[4,16]{1,0:T(4,128)(4,1)S(1)} %broadcast_in_dim.137), kind=kLoop, calls=%fused_computation.27 | loop fusion | flops 5242880 | bytes 10485888 | tf_op jit(solution)/shard_map/jit(_where)/select_n | solution.py:136
  125.8 33.6 %collective-permute-done.2 = bf16[160,26,160]{2,0,1:T(8,128)(2,1)S(1)} collective-permute-done((bf16[160,26,160]{2,0,1:T(8,128)(2,1)}, bf16[160,26,160]{2,0,1:T(8,128)(2,1)S(1)}, u32[]{:S(2)}, u32[]{:S(2)}) %collective-permute-start.2) | collective-permute-done | bytes 1331232 | tf_op jit(solution)/shard_map/ppermute | solution.py:45
  161.4 7.4 %collective-permute-done.5 = bf16[160,26,160]{2,0,1:T(8,128)(2,1)S(1)} collective-permute-done((bf16[160,26,160]{2,0,1:T(8,128)(2,1)S(1)}, bf16[160,26,160]{2,0,1:T(8,128)(2,1)S(1)}, u32[]{:S(2)}, u32[]{:S(2)}) %collective-permute-start.5) | collective-permute-done | bytes 1331232 | tf_op jit(solution)/shard_map/ppermute | solution.py:46
  169.0 5.2 %mini-gather-slice.2 = bf16[7,128,26,160]{3,1,2,0:T(8,128)(2,1)} slice(bf16[7,160,26,160]{3,1,2,0:T(8,128)(2,1)S(1)} %bitcast_dynamic-update-slice_fusion), slice={[0:7], [0:128], [0:26], [0:160]} | slice | bytes 14909440 | tf_op jit(solution)/shard_map/jit(_take)/gather | solution.py:53
  174.5 8.2 %gather_fusion.6 = bf16[4,128,26,160]{3,1,2,0:T(8,128)(2,1)} fusion(bf16[7,128,26,160]{3,1,2,0:T(8,128)(2,1)} %mini-gather-slice.2, s32[1024]{0:T(1024)S(1)} %pad_clamp_fusion.4), kind=kCustom, calls=%fused_computation.6 | custom fusion | bytes 8519696 | tf_op jit(solution)/shard_map/jit(_take)/gather | solution.py:53
  182.7 6.6 %constant_dynamic-update-slice_fusion.3 = bf16[4,160,26,160]{3,1,2,0:T(8,128)(2,1)} fusion(bf16[4,128,26,160]{3,1,2,0:T(8,128)(2,1)} %gather_fusion.6), kind=kLoop, calls=%fused_computation.111 | loop fusion | bytes 11075584
  194.1 5.4 %all-to-all-start = ((bf16[4,16,320,128]{3,2,1,0:T(8,128)(2,1)}), bf16[4,16,320,128]{3,2,1,0:T(8,128)(2,1)}, u32[]{:S(2)}, u32[]{:S(2)}) async-start(bf16[4,16,320,128]{3,2,1,0:T(8,128)(2,1)} %select_select_fusion), calls=%async_computation | async-start | bytes 10485760 | tf_op jit(solution)/shard_map/all_to_all | solution.py:192
  202.7 20.6 %collective-permute-done.7 = bf16[32,160,64]{1,2,0:T(8,128)(2,1)} collective-permute-done((bf16[32,160,64]{1,2,0:T(8,128)(2,1)}, bf16[32,160,64]{1,2,0:T(8,128)(2,1)}, u32[]{:S(2)}, u32[]{:S(2)}) %collective-permute-start.7) | collective-permute-done | bytes 655392 | tf_op jit(solution)/shard_map/ppermute | solution.py:31
  223.3 4.7 %fusion.70 = (bf16[4,160,9,160]{3,1,2,0:T(8,128)(2,1)S(1)}, bf16[4,160,9,160]{3,1,2,0:T(8,128)(2,1)}) fusion(bf16[4,160,26,160]{3,1,2,0:T(8,128)(2,1)} %constant_dynamic-update-slice_fusion.2), kind=kLoop, calls=%fused_computation.172 | loop fusion | bytes 7372800 | tf_op jit(solution)/shard_map/slice | solution.py:176
  228.1 4.2 gather_fusion.1
  232.2 7.4 %copy.66 = bf16[4,160,9,160]{1,0,3,2:T(4,128)(2,1)} copy(bf16[4,160,9,160]{3,1,2,0:T(8,128)(2,1)} %gather_fusion.1) | data formatting | bytes 3686400 | tf_op jit(solution)/shard_map/jit(_take)/gather | solution.py:176
  239.6 6.0 %reshape.458 = bf16[640,9,160,1]{0,2,1,3:T(8,128)(2,1)} reshape(bf16[4,160,9,160]{1,0,3,2:T(4,128)(2,1)} %copy.66) | data formatting | bytes 3686400 | tf_op jit(solution)/shard_map/reshape | solution.py:178
  245.6 11.4 %convolution_bitcast_fusion.1 = f32[32,9,160,8,8]{2,4,3,0,1:T(8,128)S(1)} fusion(bf16[32,160,64]{1,2,0:T(8,128)(2,1)} %collective-permute-done.8, bf16[32,160,64]{1,2,0:T(8,128)(2,1)} %collective-permute-done.7, bf16[32,160,64]{1,2,0:T(8,128)(2,1)} %collective-permute-done.6, bf16[32,160,64]{1,2,0:T(8,128)(2,1)} %fusion.36, ...), kind=kOutput, calls=%fused_computation.26 | convolution fusion | flops 3785359360 | bytes 16261120 | tf_op jit(solution)/shard_map/scq,cte->steq/dot_general | solution.py:81
  268.1 24.1 %collective-permute-done.10 = bf16[32,160,64]{1,2,0:T(8,128)(2,1)} collective-permute-done((bf16[32,160,64]{1,2,0:T(8,128)(2,1)}, bf16[32,160,64]{1,2,0:T(8,128)(2,1)}, u32[]{:S(2)}, u32[]{:S(2)}) %collective-permute-start.10) | collective-permute-done | bytes 655392 | tf_op jit(solution)/shard_map/ppermute | solution.py:31
  295.1 6.2 %copy.65 = bf16[4,160,9,160]{1,0,3,2:T(4,128)(2,1)S(1)} copy(bf16[4,160,9,160]{3,1,2,0:T(8,128)(2,1)} %gather_fusion) | data formatting | bytes 3686400 | tf_op jit(solution)/shard_map/jit(_take)/gather | solution.py:176
  304.3 11.7 %convolution_bitcast_fusion = f32[32,9,160,8,8]{2,4,3,0,1:T(8,128)S(1)} fusion(bf16[32,160,64]{1,2,0:T(8,128)(2,1)} %collective-permute-done.11, bf16[32,160,64]{1,2,0:T(8,128)(2,1)} %collective-permute-done.10, bf16[32,160,64]{1,2,0:T(8,128)(2,1)} %collective-permute-done.9, bf16[32,160,64]{1,2,0:T(8,128)(2,1)} %multiply_convert_fusion.1, ...), kind=kOutput, calls=%fused_computation.25 | convolution fusion | flops 3785359360 | bytes 16261120 | tf_op jit(solution)/shard_map/scq,cte->steq/dot_general | solution.py:81
  320.9 4.3 %all-to-all-start.2 = ((bf16[32,160,64]{1,2,0:T(8,128)(2,1)}), bf16[32,160,64]{1,2,0:T(8,128)(2,1)}, u32[]{:S(2)}, u32[]{:S(2)}) async-start(bf16[32,160,64]{1,2,0:T(8,128)(2,1)} %multiply_convert_fusion), calls=%async_computation.2 | async-start | bytes 2097152 | tf_op jit(solution)/shard_map/all_to_all | solution.py:220
  325.2 3.5 gather_fusion.4
  330.7 9.1 %all-to-all-done.2 = bf16[32,160,64]{1,2,0:T(8,128)(2,1)} async-done(((bf16[32,160,64]{1,2,0:T(8,128)(2,1)}), bf16[32,160,64]{1,2,0:T(8,128)(2,1)}, u32[]{:S(2)}, u32[]{:S(2)}) %all-to-all-start.2) | async-done | bytes 655392 | tf_op jit(solution)/shard_map/all_to_all | solution.py:220
  339.7 3.7 all-to-all-start.1
  343.7 3.5 fusion.69
  350.2 3.5 copy.72
  382.4 11.1 %convolution_convert_fusion = bf16[8,10,64,64]{3,2,1,0:T(8,128)(2,1)S(1)} fusion(bf16[8,10,64,128]{3,2,1,0:T(8,128)(2,1)} %bitcast.145, f32[8,10,64]{2,1,0:T(8,128)S(1)} %fusion.73, f32[8,10,64,128]{3,2,1,0:T(8,128)} %fusion.74, pred[8,128]{1,0:T(8,128)(4,1)S(1)} %iota_compare_fusion.4), kind=kOutput, calls=%fused_computation.94 | convolution fusion | flops 87495808 | bytes 4609024 | tf_op jit(solution)/shard_map/shqk,shdk->shdq/dot_general | solution.py:243
  397.4 13.3 %all_to_all.50 = bf16[4,2,40960]{2,1,0:T(2,128)(2,1)S(1)} all-to-all(bf16[4,2,40960]{2,1,0:T(2,128)(2,1)S(1)} %reshape.469), channel_id=1, replica_groups=mesh['groups'=2,'dp'=4,'mp'=4] {'mp'}, dimensions={0} | all-to-all | bytes 1310720 | tf_op jit(solution)/shard_map/all_to_all | solution.py:249
  412.4 3.5 copy.78
  415.9 3.5 fusion.38
  (151 shorter events, 101.0 us)
Async XLA Ops:
  0.0 67.7 %copy-start = (bf16[42,320,128]{2,1,0:T(8,128)(2,1)S(1)}, bf16[42,320,128]{2,1,0:T(8,128)(2,1)}, u32[]{:S(2)}) copy-start(bf16[42,320,128]{2,1,0:T(8,128)(2,1)} %param.14) | copy-start | bytes 10321924
  6.0 3.9 copy-start.7
  6.0 12.3 %copy-start.3 = (bf16[32,160,64]{1,2,0:T(8,128)(2,1)S(1)}, bf16[32,160,64]{1,2,0:T(8,128)(2,1)}, u32[]{:S(2)}) copy-start(bf16[32,160,64]{1,2,0:T(8,128)(2,1)} %param.10) | copy-start | bytes 1966084
  9.9 17.4 %copy-start.9 = (s32[128]{0:T(128)S(1)}, s32[128]{0:T(128)}, u32[]{:S(2)}) copy-start(s32[128]{0:T(128)} %param.18) | copy-start | bytes 1540
  9.9 57.3 %copy-start.10 = (s32[128]{0:T(128)S(1)}, s32[128]{0:T(128)}, u32[]{:S(2)}) copy-start(s32[128]{0:T(128)} %param.17) | copy-start | bytes 1540
  10.7 50.8 %collective-permute-start = (bf16[160,26,160]{2,0,1:T(8,128)(2,1)}, bf16[160,26,160]{2,0,1:T(8,128)(2,1)}, u32[]{:S(2)}, u32[]{:S(2)}) collective-permute-start(bf16[160,26,160]{2,0,1:T(8,128)(2,1)} %copy_dynamic-update-slice_fusion), channel_id=1, source_target_pairs={{0,4},{4,8},{8,12},{1,5},{5,9},{9,13},{2,6},{6,10},{10,14},{3,7},{... | collective-permute-start | bytes 3993608 | tf_op jit(solution)/shard_map/ppermute | solution.py:45
  17.0 54.2 %collective-permute-start.3 = (bf16[160,26,160]{2,0,1:T(8,128)(2,1)}, bf16[160,26,160]{2,0,1:T(8,128)(2,1)}, u32[]{:S(2)}, u32[]{:S(2)}) collective-permute-start(bf16[160,26,160]{2,0,1:T(8,128)(2,1)} %copy_dynamic-update-slice_fusion), channel_id=1, source_target_pairs={{4,0},{8,4},{12,8},{5,1},{9,5},{13,9},{6,2},{10,6},{14,10},{7,3},{... | collective-permute-start | bytes 3993608 | tf_op jit(solution)/shard_map/ppermute | solution.py:46
  61.5 49.4 %collective-permute-start.1 = (bf16[160,26,160]{2,0,1:T(8,128)(2,1)}, bf16[160,26,160]{2,0,1:T(8,128)(2,1)}, u32[]{:S(2)}, u32[]{:S(2)}) collective-permute-start(bf16[160,26,160]{2,0,1:T(8,128)(2,1)} %collective-permute-done), channel_id=1, source_target_pairs={{0,4},{4,8},{8,12},{1,5},{5,9},{9,13},{2,6},{6,10},{10,14},{3,7},{... | collective-permute-start | bytes 3993608 | tf_op jit(solution)/shard_map/ppermute | solution.py:45
  71.2 49.8 %collective-permute-start.4 = (bf16[160,26,160]{2,0,1:T(8,128)(2,1)}, bf16[160,26,160]{2,0,1:T(8,128)(2,1)S(1)}, u32[]{:S(2)}, u32[]{:S(2)}) collective-permute-start(bf16[160,26,160]{2,0,1:T(8,128)(2,1)} %collective-permute-done.3), channel_id=1, source_target_pairs={{4,0},{8,4},{12,8},{5,1},{9,5},{13,9},{6,2},{10,6},{14,10},{7,3},{... | collective-permute-start | bytes 3993608 | tf_op jit(solution)/shard_map/ppermute | solution.py:46
  110.9 48.5 %collective-permute-start.2 = (bf16[160,26,160]{2,0,1:T(8,128)(2,1)}, bf16[160,26,160]{2,0,1:T(8,128)(2,1)S(1)}, u32[]{:S(2)}, u32[]{:S(2)}) collective-permute-start(bf16[160,26,160]{2,0,1:T(8,128)(2,1)} %collective-permute-done.1), channel_id=1, source_target_pairs={{0,4},{4,8},{8,12},{1,5},{5,9},{9,13},{2,6},{6,10},{10,14},{3,7},{... | collective-permute-start | bytes 3993608 | tf_op jit(solution)/shard_map/ppermute | solution.py:45
  121.0 47.9 %collective-permute-start.5 = (bf16[160,26,160]{2,0,1:T(8,128)(2,1)S(1)}, bf16[160,26,160]{2,0,1:T(8,128)(2,1)S(1)}, u32[]{:S(2)}, u32[]{:S(2)}) collective-permute-start(bf16[160,26,160]{2,0,1:T(8,128)(2,1)S(1)} %collective-permute-done.4), channel_id=1, source_target_pairs={{4,0},{8,4},{12,8},{5,1},{9,5},{13,9},{6,2},{10,6},{14,10},{7,3},{... | collective-permute-start | bytes 3993608 | tf_op jit(solution)/shard_map/ppermute | solution.py:46
  194.1 5.4 %copy-start.4 = (bf16[32,160,64]{1,2,0:T(8,128)(2,1)S(1)}, bf16[32,160,64]{1,2,0:T(8,128)(2,1)}, u32[]{:S(2)}) copy-start(bf16[32,160,64]{1,2,0:T(8,128)(2,1)} %param.10) | copy-start | bytes 1966084
  194.1 126.9 %all-to-all-start = ((bf16[4,16,320,128]{3,2,1,0:T(8,128)(2,1)}), bf16[4,16,320,128]{3,2,1,0:T(8,128)(2,1)}, u32[]{:S(2)}, u32[]{:S(2)}) async-start(bf16[4,16,320,128]{3,2,1,0:T(8,128)(2,1)} %select_select_fusion), calls=%async_computation | async-start | bytes 10485760 | tf_op jit(solution)/shard_map/all_to_all | solution.py:192
  199.5 3.1 copy-start.8
  201.1 22.2 %collective-permute-start.7 = (bf16[32,160,64]{1,2,0:T(8,128)(2,1)}, bf16[32,160,64]{1,2,0:T(8,128)(2,1)}, u32[]{:S(2)}, u32[]{:S(2)}) collective-permute-start(bf16[32,160,64]{1,2,0:T(8,128)(2,1)} %fusion.36), channel_id=1, source_target_pairs={{0,2},{1,3},{2,0},{3,1},{4,6},{5,7},{6,4},{7,5},{8,10},{9,11},{10,... | collective-permute-start | bytes 1966088 | tf_op jit(solution)/shard_map/ppermute | solution.py:31
  202.6 43.0 %collective-permute-start.6 = (bf16[32,160,64]{1,2,0:T(8,128)(2,1)}, bf16[32,160,64]{1,2,0:T(8,128)(2,1)}, u32[]{:S(2)}, u32[]{:S(2)}) collective-permute-start(bf16[32,160,64]{1,2,0:T(8,128)(2,1)} %fusion.36), channel_id=1, source_target_pairs={{0,1},{1,0},{2,3},{3,2},{4,5},{5,4},{6,7},{7,6},{8,9},{9,8},{10,11... | collective-permute-start | bytes 1966088 | tf_op jit(solution)/shard_map/ppermute | solution.py:32
  223.3 22.3 %collective-permute-start.8 = (bf16[32,160,64]{1,2,0:T(8,128)(2,1)}, bf16[32,160,64]{1,2,0:T(8,128)(2,1)}, u32[]{:S(2)}, u32[]{:S(2)}) collective-permute-start(bf16[32,160,64]{1,2,0:T(8,128)(2,1)} %collective-permute-done.7), channel_id=1, source_target_pairs={{0,1},{1,0},{2,3},{3,2},{4,5},{5,4},{6,7},{7,6},{8,9},{9,8},{10,11... | collective-permute-start | bytes 1966088 | tf_op jit(solution)/shard_map/ppermute | solution.py:33
  266.3 25.9 %collective-permute-start.10 = (bf16[32,160,64]{1,2,0:T(8,128)(2,1)}, bf16[32,160,64]{1,2,0:T(8,128)(2,1)}, u32[]{:S(2)}, u32[]{:S(2)}) collective-permute-start(bf16[32,160,64]{1,2,0:T(8,128)(2,1)} %multiply_convert_fusion.1), channel_id=1, source_target_pairs={{0,2},{1,3},{2,0},{3,1},{4,6},{5,7},{6,4},{7,5},{8,10},{9,11},{10,... | collective-permute-start | bytes 1966088 | tf_op jit(solution)/shard_map/ppermute | solution.py:31
  267.9 36.4 %collective-permute-start.9 = (bf16[32,160,64]{1,2,0:T(8,128)(2,1)}, bf16[32,160,64]{1,2,0:T(8,128)(2,1)}, u32[]{:S(2)}, u32[]{:S(2)}) collective-permute-start(bf16[32,160,64]{1,2,0:T(8,128)(2,1)} %multiply_convert_fusion.1), channel_id=1, source_target_pairs={{0,1},{1,0},{2,3},{3,2},{4,5},{5,4},{6,7},{7,6},{8,9},{9,8},{10,11... | collective-permute-start | bytes 1966088 | tf_op jit(solution)/shard_map/ppermute | solution.py:32
  292.2 12.1 %collective-permute-start.11 = (bf16[32,160,64]{1,2,0:T(8,128)(2,1)}, bf16[32,160,64]{1,2,0:T(8,128)(2,1)}, u32[]{:S(2)}, u32[]{:S(2)}) collective-permute-start(bf16[32,160,64]{1,2,0:T(8,128)(2,1)} %collective-permute-done.10), channel_id=1, source_target_pairs={{0,1},{1,0},{2,3},{3,2},{4,5},{5,4},{6,7},{7,6},{8,9},{9,8},{10,11... | collective-permute-start | bytes 1966088 | tf_op jit(solution)/shard_map/ppermute | solution.py:33
  304.3 11.7 %copy-start.5 = (bf16[32,160,64]{1,2,0:T(8,128)(2,1)S(1)}, bf16[32,160,64]{1,2,0:T(8,128)(2,1)}, u32[]{:S(2)}) copy-start(bf16[32,160,64]{1,2,0:T(8,128)(2,1)} %param.10) | copy-start | bytes 1966084
  318.4 2.6 copy-start.2
  320.9 18.8 %all-to-all-start.2 = ((bf16[32,160,64]{1,2,0:T(8,128)(2,1)}), bf16[32,160,64]{1,2,0:T(8,128)(2,1)}, u32[]{:S(2)}, u32[]{:S(2)}) async-start(bf16[32,160,64]{1,2,0:T(8,128)(2,1)} %multiply_convert_fusion), calls=%async_computation.2 | async-start | bytes 2097152 | tf_op jit(solution)/shard_map/all_to_all | solution.py:220
  330.7 12.7 %copy-start.11 = (s32[168]{0:T(256)S(1)}, s32[168]{0:T(256)}, u32[]{:S(2)}) copy-start(s32[168]{0:T(256)} %param.19) | copy-start | bytes 2020
  339.7 36.7 %all-to-all-start.1 = ((bf16[32,320,128]{2,1,0:T(8,128)(2,1)}), bf16[32,320,128]{2,1,0:T(8,128)(2,1)S(1)}, u32[]{:S(2)}, u32[]{:S(2)}) async-start(bf16[32,320,128]{2,1,0:T(8,128)(2,1)} %broadcast_select_fusion), calls=%async_computation.1 | async-start | bytes 5242880 | tf_op jit(solution)/shard_map/all_to_all | solution.py:221
  376.7 1.7 copy-start.6
  412.4 7.1 %copy-start.1 = (bf16[42,320,128]{2,1,0:T(8,128)(2,1)S(1)}, bf16[42,320,128]{2,1,0:T(8,128)(2,1)}, u32[]{:S(2)}) copy-start(bf16[42,320,128]{2,1,0:T(8,128)(2,1)} %param.14) | copy-start | bytes 10321924
